TPU v7x, 128 devices: a whole 4x4x4 slice. The times are simulated.
128 devices in a mesh: outer: 8 (over z, core), inner: 16 (over x, y).
Axes of the slice: x: 4, y: 4, z: 4, core: 2. Of those that a mesh axis runs over, the one named last changes fastest.
Arguments:
- child_update: float32 [8, 2048, 2048], P('outer', 'inner'), may hold values from -1 to 8, as said below
- block_map: int32 [2, 8, 16], replicated, may hold values from 0 to 23, as said below
- obs_design: bfloat16 [262144, 128], P(('outer', 'inner')), may hold values from -2 to 2
- obs_target: int32 [262144], P(('outer', 'inner')), may hold values from 0 to 47
Outputs:
- pivot_factor: float32 [2, 8, 1024, 1024], P(None, 'outer', 'inner')
- border_factor: float32 [2, 8, 2048, 1024], P(None, 'outer', 'inner')
- top_update: float32 [8, 2048, 2048], P('outer', 'inner')
Inputs may be any that keep to these rules, and one draw needn't show every extreme that they name: `child_update`: each group's matrix is symmetric and positive definite. `block_map`: entry [l, g] names distinct parent blocks for the blocks of one child; groups under the same child hold equal entries; the two children of a parent together name every parent block.
All inputs are finite; a program needn't handle non-finite values.
Results may differ from a plain program's by a relative error of at most 0.0003.
Values sent between devices are 32-bit elements; how exact they have to be, the bound alone decides.
No kernel may reach another device: no remote copies, remote signals or barrier semaphores. Data moves between devices by JAX's collectives and lax.ppermute only.
A program may use at most 128 MiB of HBM per device.

v0:
```python
import math
import jax
import jax.numpy as jnp
from jax import lax
from jax.sharding import PartitionSpec as P

S = 1024
B = 2048
BLK = 128
LEVELS = 2
HIGHEST = lax.Precision.HIGHEST


def partner_2(block, axis, bit):
    count = lax.axis_size(axis)
    route = []
    for low in range(count):
        high = low | 1 << bit
        if high != low and high < count:
            route += [(low, high), (high, low)]
    return lax.ppermute(block, axis, route)


def block_source(child_map, parent_count):
    child_count = child_map.shape[0]
    matches = child_map[:, None] == jnp.arange(parent_count, dtype=jnp.int32)[None, :]
    source = jnp.sum(
        jnp.where(matches, jnp.arange(child_count, dtype=jnp.int32)[:, None], 0), axis=0
    )
    present = jnp.any(matches, axis=0)
    return (source, present)


def parent_columns(child_rows, child_map, parent_count):
    row_count = child_rows.shape[0]
    child_count = child_map.shape[0]
    block_size = child_rows.shape[1] // child_count
    source, present = block_source(child_map, parent_count)
    blocks = child_rows.reshape(row_count, child_count, block_size)
    picked = jnp.take(blocks, source, axis=1)
    picked = jnp.where(present[None, :, None], picked, jnp.zeros_like(picked))
    return picked.reshape(row_count, parent_count * block_size)


def parent_rows(child_cols, child_map, parent_count):
    col_count = child_cols.shape[1]
    child_count = child_map.shape[0]
    block_size = child_cols.shape[0] // child_count
    source, present = block_source(child_map, parent_count)
    blocks = child_cols.reshape(child_count, block_size, col_count)
    picked = jnp.take(blocks, source, axis=0)
    picked = jnp.where(present[:, None, None], picked, jnp.zeros_like(picked))
    return picked.reshape(parent_count * block_size, col_count)


def owner_major(parent_cols, inner_count):
    row_count = parent_cols.shape[0]
    sep_part = parent_cols[:, :S].reshape(row_count, inner_count, S // inner_count)
    border_part = parent_cols[:, S:].reshape(row_count, inner_count, B // inner_count)
    return jnp.concatenate([sep_part, border_part], axis=2)


def blocked_cholesky(matrix, panel_size):
    order = matrix.shape[0]
    lower_factor = jnp.zeros_like(matrix)
    trailing = matrix
    inverse_list = []
    for panel_index in range(order // panel_size):
        first = panel_index * panel_size
        last = first + panel_size
        diagonal_block = trailing[first:last, first:last]
        panel_lower = jnp.linalg.cholesky(diagonal_block)
        identity = jnp.eye(panel_size, dtype=jnp.float32)
        inverse = jax.scipy.linalg.solve_triangular(panel_lower, identity, lower=True)
        inverse_list.append(inverse)
        lower_factor = lower_factor.at[first:last, first:last].set(panel_lower)
        if last < order:
            below = jnp.dot(
                trailing[last:, first:last],
                inverse.T,
                precision=HIGHEST,
                preferred_element_type=jnp.float32,
            )
            lower_factor = lower_factor.at[last:, first:last].set(below)
            update = jnp.dot(below, below.T, precision=HIGHEST, preferred_element_type=jnp.float32)
            trailing = trailing.at[last:, last:].add(-update)
    return (lower_factor, inverse_list)


def cholesky_inverse(matrix, base_size):
    order = matrix.shape[0]
    if order <= base_size:
        lower = jnp.linalg.cholesky(matrix)
        identity = jnp.eye(order, dtype=jnp.float32)
        return (lower, jax.scipy.linalg.solve_triangular(lower, identity, lower=True))
    half = order // 2
    lower_11, inverse_11 = cholesky_inverse(matrix[:half, :half], base_size)
    lower_21 = jnp.dot(
        matrix[half:, :half], inverse_11.T, precision=HIGHEST, preferred_element_type=jnp.float32
    )
    schur = matrix[half:, half:] - jnp.dot(
        lower_21, lower_21.T, precision=HIGHEST, preferred_element_type=jnp.float32
    )
    lower_22, inverse_22 = cholesky_inverse(schur, base_size)
    inverse_21 = -jnp.dot(
        inverse_22,
        jnp.dot(lower_21, inverse_11, precision=HIGHEST, preferred_element_type=jnp.float32),
        precision=HIGHEST,
        preferred_element_type=jnp.float32,
    )
    zero = jnp.zeros((half, half), jnp.float32)
    lower = jnp.block([[lower_11, zero], [lower_21, lower_22]])
    inverse = jnp.block([[inverse_11, zero], [inverse_21, inverse_22]])
    return (lower, inverse)


def border_solve(rows_in, lower_factor, inverse_list, panel_size):
    solved = []
    for panel_index in range(len(inverse_list)):
        first = panel_index * panel_size
        pending = rows_in[:, first : first + panel_size]
        for earlier in range(panel_index):
            coupling = lower_factor[
                first : first + panel_size, earlier * panel_size : (earlier + 1) * panel_size
            ]
            pending = pending - jnp.dot(
                solved[earlier], coupling.T, precision=HIGHEST, preferred_element_type=jnp.float32
            )
        solved.append(
            jnp.dot(
                pending,
                inverse_list[panel_index].T,
                precision=HIGHEST,
                preferred_element_type=jnp.float32,
            )
        )
    return jnp.concatenate(solved, axis=1)


def shards(child_update, block_map, obs_design, obs_target):
    inner_count = lax.axis_size("inner")
    group_count = lax.axis_size("outer")
    group_index = lax.axis_index("outer")
    member = lax.axis_index("inner")
    parent_count = (S + B) // BLK
    sep_rows = S // inner_count
    sep_blocks = S // BLK
    panel_size = min(S, 256)
    front_total = sum((group_count >> level_index + 1 for level_index in range(LEVELS)))
    target_total = front_total * sep_blocks
    row_count = obs_design.shape[0]
    step_rows = math.gcd(row_count, 256)
    target_ids = jnp.arange(target_total, dtype=jnp.int32)

    def add_rows(block_index, running):
        design = lax.dynamic_slice_in_dim(obs_design, block_index * step_rows, step_rows, 0)
        labels = lax.dynamic_slice_in_dim(obs_target, block_index * step_rows, step_rows, 0)
        selector = (labels[:, None] == target_ids[None, :]).astype(jnp.bfloat16)
        spread = selector[:, :, None] * design[:, None, :]
        return running + jnp.einsum(
            "rtj,rk->tjk", spread, design, preferred_element_type=jnp.float32
        )

    gram_blocks = lax.fori_loop(
        0, row_count // step_rows, add_rows, jnp.zeros((target_total, BLK, BLK), jnp.float32)
    )
    per_front = gram_blocks.reshape(front_total, S, BLK)
    obs_share = lax.psum(
        lax.psum_scatter(per_front, "inner", scatter_dimension=1, tiled=True), "outer"
    )
    current = child_update[0]
    pivot_list = []
    border_list = []
    front_offset = 0
    block_start = member * sep_rows // BLK * BLK
    for level_index in range(LEVELS):
        partner = group_index ^ 1 << level_index
        level_maps = block_map[level_index]
        own_map = lax.dynamic_index_in_dim(level_maps, group_index, 0, keepdims=False)
        sib_map = lax.dynamic_index_in_dim(level_maps, partner, 0, keepdims=False)
        sibling = partner_2(current, "outer", level_index)
        outgoing = jnp.stack(
            [
                owner_major(parent_columns(current, own_map, parent_count), inner_count),
                owner_major(parent_columns(sibling, sib_map, parent_count), inner_count),
            ]
        )
        arrived = lax.all_to_all(outgoing, "inner", split_axis=2, concat_axis=1, tiled=True)
        own_cols = parent_rows(arrived[0, :, 0, :], own_map, parent_count)
        sib_cols = parent_rows(arrived[1, :, 0, :], sib_map, parent_count)
        front_rows = (own_cols + sib_cols).T
        front_slot = front_offset + (group_index >> level_index + 1)
        obs_rows = lax.dynamic_index_in_dim(obs_share, front_slot, 0, keepdims=False)
        sep_front = front_rows[:sep_rows]
        block_now = lax.dynamic_slice_in_dim(sep_front, block_start, BLK, 1)
        sep_front = lax.dynamic_update_slice_in_dim(sep_front, block_now + obs_rows, block_start, 1)
        front_offset = front_offset + (group_count >> level_index + 1)
        pivot_all = lax.all_gather(sep_front[:, :S], "inner", axis=0, tiled=True)
        border_front = front_rows[sep_rows:]
        coupling_all = lax.all_gather(border_front[:, :S], "inner", axis=0, tiled=True)
        pivot_lower, pivot_inverse = cholesky_inverse(pivot_all, BLK)
        border_all = jnp.dot(
            coupling_all, pivot_inverse.T, precision=HIGHEST, preferred_element_type=jnp.float32
        )
        border_factor = lax.dynamic_slice_in_dim(
            border_all, member * (B // inner_count), B // inner_count, 0
        )
        product = jnp.einsum(
            "rs,cs->rc",
            border_factor,
            border_all,
            precision=HIGHEST,
            preferred_element_type=jnp.float32,
        )
        current = border_front[:, S:] - product
        pivot_list.append(lax.dynamic_slice_in_dim(pivot_lower, member * sep_rows, sep_rows, 0))
        border_list.append(border_factor)
    pivot_factor = jnp.stack(pivot_list)[:, None]
    border_out = jnp.stack(border_list)[:, None]
    return (pivot_factor, border_out, current[None])


def solution(mesh):
    in_specs = (P("outer", "inner", None), P(), P(("outer", "inner"), None), P(("outer", "inner")))
    out_specs = (
        P(None, "outer", "inner", None),
        P(None, "outer", "inner", None),
        P("outer", "inner", None),
    )
    return jax.shard_map(shards, mesh=mesh, in_specs=in_specs, out_specs=out_specs, check_vma=False)
```

profile of v0, /device:TPU:1, one launch (start us, length us, event | category | flops | bytes accessed | tf_op | source)
XLA Modules:
  0.0 1052.3 jit_solution(1851597873496397429)
XLA Ops:
  7.2 2.5 copy.410
  11.1 25.9 %while.14 = (s32[]{:T(128)}, f32[48,128,128]{2,1,0:T(8,128)S(1)}, s32[2048]{0:T(1024)}, bf16[2048,128]{1,0:T(8,128)(2,1)}, s32[]{:T(128)}, /*index=5*/s32[]{:T(128)}, s32[]{:T(128)}, s32[]{:T(128)}) while((s32[]{:T(128)}, f32[48,128,128]{2,1,0:T(8,128)S(1)}, s32[2048]{0:T(1024)}, bf16[2048,128]{1,0:T(8,128)(2,1)}, s32[]{:T(128)}, ...), condition=%wide.region_5.8_spmd.clone, body=%wide.region_4.7_spmd.clone.sunk | while | flops 405823488 | bytes 6737053 | solution.py:164
  37.0 3.9 copy.418
  57.3 6.8 all-to-all-start
  64.3 46.5 %all-to-all-done = f32[2,128,16,192]{1,3,0,2:T(8,128)S(1)} async-done(((f32[2,128,16,192]{1,3,0,2:T(8,128)}), f32[2,128,16,192]{1,3,0,2:T(8,128)S(1)}, u32[]{:S(2)}, u32[]{:S(2)}) %all-to-all-start) | async-done | bytes 3145760 | tf_op jit(solution)/shard_map/all_to_all | solution.py:188
  111.3 2.2 gather_fusion.2
  113.4 2.2 gather_fusion.3
  115.6 39.2 %reduce-scatter.2.cloned.1.call-done = f32[6,64,128]{2,0,1:T(8,128)} async-done(((f32[6,1024,128]{2,0,1:T(8,128)}), f32[6,64,128]{2,0,1:T(8,128)}) %reduce-scatter.2.cloned.1.call-update) | async-done | bytes 196624 | tf_op jit(solution)/shard_map/reduce_scatter | solution.py:169
  154.8 2.8 bitcast_bitcast_fusion.1
  157.8 58.7 %all-reduce.30.cloned.1.call-done = f32[6,64,128]{2,0,1:T(8,128)} async-done(((f32[6,64,128]{2,0,1:T(8,128)}), f32[6,64,128]{2,0,1:T(8,128)}) %all-reduce.30.cloned.1.call-update) | async-done | bytes 196624 | tf_op jit(solution)/shard_map/psum | solution.py:168
  221.2 50.2 %all-gather.5.cloned.1.call-done = f32[1024,1024]{1,0:T(8,128)} async-done(((f32[64,1024]{1,0:T(8,128)}), f32[1024,1024]{1,0:T(8,128)}) %all-gather.5.cloned.1.call-update) | async-done | bytes 4194320 | tf_op jit(solution)/shard_map/all_gather | solution.py:198
  273.3 11.7 %cholesky.254 = f32[128,128]{1,0:T(8,128)S(1)} custom-call(f32[128,128]{1,0:T(8,128)S(1)} %get-tuple-element.171), custom_call_target="Cholesky" | custom-call | tf_op jit(solution)/shard_map/jit(cholesky)/cholesky | solution.py:93
  287.0 9.8 custom-call.21
  298.6 11.7 %cholesky.265 = f32[128,128]{1,0:T(8,128)S(1)} custom-call(f32[128,128]{1,0:T(8,128)S(1)} %fusion.203), custom_call_target="Cholesky" | custom-call | tf_op jit(solution)/shard_map/jit(cholesky)/cholesky | solution.py:93
  312.3 9.9 custom-call.22
  326.5 11.7 %cholesky.276 = f32[128,128]{1,0:T(8,128)S(1)} custom-call(f32[128,128]{1,0:T(8,128)S(1)} %fusion.201), custom_call_target="Cholesky" | custom-call | tf_op jit(solution)/shard_map/jit(cholesky)/cholesky | solution.py:93
  340.2 9.8 custom-call.23
  350.9 11.9 %cholesky.287 = f32[128,128]{1,0:T(8,128)S(1)} custom-call(f32[128,128]{1,0:T(8,128)S(1)} %fusion.199), custom_call_target="Cholesky" | custom-call | tf_op jit(solution)/shard_map/jit(cholesky)/cholesky | solution.py:93
  364.8 9.8 custom-call.24
  375.0 2.3 slice.307
  377.4 2.5 copy.530
  382.3 3.1 fusion.51
  391.3 12.9 %cholesky.298 = f32[128,128]{1,0:T(8,128)S(1)} custom-call(f32[128,128]{1,0:T(8,128)} %fusion.197), custom_call_target="Cholesky" | custom-call | tf_op jit(solution)/shard_map/jit(cholesky)/cholesky | solution.py:93
  406.1 11.3 %custom-call.25 = f32[1,128,128]{1,2,0:T(8,128)} custom-call(f32[1,128,128]{2,1,0:T(8,128)} %get-tuple-element.158), custom_call_target="InvertDiagBlocksLowerTriangular" | custom-call | tf_op jit(solution)/shard_map/jit(_solve_triangular)/triangular_solve | solution.py:95
  425.0 13.2 %cholesky.309 = f32[128,128]{1,0:T(8,128)} custom-call(f32[128,128]{1,0:T(8,128)} %fusion.195), custom_call_target="Cholesky" | custom-call | tf_op jit(solution)/shard_map/jit(cholesky)/cholesky | solution.py:93
  439.8 2.2 select_bitcast_fusion.10
  442.0 11.3 %custom-call.26 = f32[1,128,128]{1,2,0:T(8,128)} custom-call(f32[1,128,128]{2,1,0:T(8,128)} %get-tuple-element.156), custom_call_target="InvertDiagBlocksLowerTriangular" | custom-call | tf_op jit(solution)/shard_map/jit(_solve_triangular)/triangular_solve | solution.py:95
  467.4 13.3 %cholesky.320 = f32[128,128]{1,0:T(8,128)} custom-call(f32[128,128]{1,0:T(8,128)} %fusion.193), custom_call_target="Cholesky" | custom-call | tf_op jit(solution)/shard_map/jit(cholesky)/cholesky | solution.py:93
  482.3 2.2 select_bitcast_fusion.9
  484.5 11.3 %custom-call.27 = f32[1,128,128]{1,2,0:T(8,128)} custom-call(f32[1,128,128]{2,1,0:T(8,128)} %get-tuple-element.154), custom_call_target="InvertDiagBlocksLowerTriangular" | custom-call | tf_op jit(solution)/shard_map/jit(_solve_triangular)/triangular_solve | solution.py:95
  504.1 13.2 %cholesky.331 = f32[128,128]{1,0:T(8,128)} custom-call(f32[128,128]{1,0:T(8,128)} %fusion.191), custom_call_target="Cholesky" | custom-call | tf_op jit(solution)/shard_map/jit(cholesky)/cholesky | solution.py:93
  520.9 11.3 %custom-call.28 = f32[1,128,128]{1,2,0:T(8,128)} custom-call(f32[1,128,128]{2,1,0:T(8,128)} %get-tuple-element.152), custom_call_target="InvertDiagBlocksLowerTriangular" | custom-call | tf_op jit(solution)/shard_map/jit(_solve_triangular)/triangular_solve | solution.py:95
  536.8 2.4 select_maximum_fusion.6
  543.8 2.9 convolution_negate_fusion.1
  546.7 36.2 %fusion.12 = f32[2048,1024]{1,0:T(8,128)S(1)} fusion(f32[2048,1024]{1,0:T(8,128)} %all-gather.7.cloned.1.call-done, f32[512,512]{1,0:T(8,128)S(1)} %copy-done.37, f32[128,128]{1,0:T(8,128)S(1)} %copy-done.85, f32[128,128]{1,0:T(8,128)} %copy-done.81, f32[128,256]{1,0:T(8,128)} %concatenate.310, f32[256,256]{1,0:T(8,128)} %copy-done.77, ...), kind=kOutput, calls=%fused_computation.29 | convolution fusion | flops 25778192384 | bytes 19922944 | tf_op jit(solution)/shard_map/dot_general | solution.py:202
  582.9 9.7 convolution_subtract_fusion.1
  600.7 16.1 %collective-permute-done.1 = f32[128,2048]{1,0:T(8,128)} collective-permute-done((f32[128,2048]{1,0:T(8,128)}, f32[128,2048]{1,0:T(8,128)}, u32[]{:S(2)}, u32[]{:S(2)}) %collective-permute-start.1) | collective-permute-done | bytes 1048608 | tf_op jit(solution)/shard_map/ppermute | solution.py:21
  623.8 42.2 %all_to_all.30 = f32[2,128,16,192]{1,3,0,2:T(8,128)S(1)} all-to-all(f32[2,128,16,192]{1,3,0,2:T(8,128)S(1)} %pad_maximum_fusion.1), channel_id=1, replica_groups=mesh['outer'=8,'inner'=16] {'inner'}, dimensions={2} | all-to-all | bytes 6291456 | tf_op jit(solution)/shard_map/all_to_all | solution.py:188
  670.8 2.9 bitcast_bitcast_fusion
  692.2 2.5 pad_select_fusion.1
  696.5 29.6 %all-gather.9.cloned.1.call-done = f32[1024,1024]{1,0:T(8,128)} async-done(((f32[64,1024]{1,0:T(8,128)}), f32[1024,1024]{1,0:T(8,128)}) %all-gather.9.cloned.1.call-update) | async-done | bytes 4194320 | tf_op jit(solution)/shard_map/all_gather | solution.py:198
  728.1 11.7 %cholesky.342 = f32[128,128]{1,0:T(8,128)S(1)} custom-call(f32[128,128]{1,0:T(8,128)S(1)} %get-tuple-element.169), custom_call_target="Cholesky" | custom-call | tf_op jit(solution)/shard_map/jit(cholesky)/cholesky | solution.py:93
  741.9 9.8 custom-call.29
  754.2 11.9 %cholesky.353 = f32[128,128]{1,0:T(8,128)S(1)} custom-call(f32[128,128]{1,0:T(8,128)S(1)} %fusion.187), custom_call_target="Cholesky" | custom-call | tf_op jit(solution)/shard_map/jit(cholesky)/cholesky | solution.py:93
  768.1 9.8 custom-call.30
  783.0 11.7 %cholesky.364 = f32[128,128]{1,0:T(8,128)S(1)} custom-call(f32[128,128]{1,0:T(8,128)S(1)} %fusion.185), custom_call_target="Cholesky" | custom-call | tf_op jit(solution)/shard_map/jit(cholesky)/cholesky | solution.py:93
  796.7 9.8 custom-call.31
  808.2 12.1 %cholesky.375 = f32[128,128]{1,0:T(8,128)S(1)} custom-call(f32[128,128]{1,0:T(8,128)S(1)} %fusion.183), custom_call_target="Cholesky" | custom-call | tf_op jit(solution)/shard_map/jit(cholesky)/cholesky | solution.py:93
  822.2 9.8 custom-call.32
  832.4 2.3 slice.335
  834.7 2.6 copy.534
  839.7 3.1 fusion.47
  844.1 3.1 convolution_subtract_fusion.2
  849.2 11.9 %cholesky.386 = f32[128,128]{1,0:T(8,128)S(1)} custom-call(f32[128,128]{1,0:T(8,128)S(1)} %fusion.181), custom_call_target="Cholesky" | custom-call | tf_op jit(solution)/shard_map/jit(cholesky)/cholesky | solution.py:93
  863.2 10.4 custom-call.33
  881.3 13.2 %cholesky.397 = f32[128,128]{1,0:T(8,128)} custom-call(f32[128,128]{1,0:T(8,128)} %fusion.179), custom_call_target="Cholesky" | custom-call | tf_op jit(solution)/shard_map/jit(cholesky)/cholesky | solution.py:93
  898.2 11.3 %custom-call.34 = f32[1,128,128]{1,2,0:T(8,128)} custom-call(f32[1,128,128]{2,1,0:T(8,128)} %get-tuple-element.140), custom_call_target="InvertDiagBlocksLowerTriangular" | custom-call | tf_op jit(solution)/shard_map/jit(_solve_triangular)/triangular_solve | solution.py:95
  924.3 12.5 %cholesky.408 = f32[128,128]{1,0:T(8,128)S(1)} custom-call(f32[128,128]{1,0:T(8,128)} %fusion.177), custom_call_target="Cholesky" | custom-call | tf_op jit(solution)/shard_map/jit(cholesky)/cholesky | solution.py:93
  938.7 10.6 %custom-call.35 = f32[1,128,128]{1,2,0:T(8,128)S(1)} custom-call(f32[1,128,128]{2,1,0:T(8,128)} %get-tuple-element.138), custom_call_target="InvertDiagBlocksLowerTriangular" | custom-call | tf_op jit(solution)/shard_map/jit(_solve_triangular)/triangular_solve | solution.py:95
  956.9 13.2 %cholesky.419 = f32[128,128]{1,0:T(8,128)} custom-call(f32[128,128]{1,0:T(8,128)} %fusion.175), custom_call_target="Cholesky" | custom-call | tf_op jit(solution)/shard_map/jit(cholesky)/cholesky | solution.py:93
  974.1 11.3 %custom-call.36 = f32[1,128,128]{1,2,0:T(8,128)} custom-call(f32[1,128,128]{2,1,0:T(8,128)} %get-tuple-element.136), custom_call_target="InvertDiagBlocksLowerTriangular" | custom-call | tf_op jit(solution)/shard_map/jit(_solve_triangular)/triangular_solve | solution.py:95
  1000.9 2.8 convolution_negate_fusion
  1003.8 30.6 %fusion.10 = f32[2048,1024]{1,0:T(8,128)S(1)} fusion(f32[2048,1024]{1,0:T(8,128)} %all-gather.11.cloned.1.call-done, f32[512,512]{1,0:T(8,128)S(1)} %copy-done.36, f32[128,128]{1,0:T(8,128)} %copy.496, f32[128,128]{1,0:T(8,128)} %copy-done.80, f32[128,256]{1,0:T(8,128)S(1)} %copy-done.67, f32[256,256]{1,0:T(8,128)} %copy-done.76, ...), kind=kOutput, calls=%fused_computation.23 | convolution fusion | flops 25778192384 | bytes 19922944 | tf_op jit(solution)/shard_map/dot_general | solution.py:202
  1034.4 9.7 fusion.38
  (511 shorter events, 244.0 us)
Async XLA Ops:
  7.2 147.6 %reduce-scatter.2.cloned.1.call-start = ((), (), s32[]{:S(2)}) async-start(), calls=%async_computation.3 | async-start | bytes 4456448 | tf_op jit(solution)/shard_map/reduce_scatter | solution.py:169
  9.7 38.6 %collective-permute-start = (f32[128,2048]{0,1:T(8,128)}, f32[128,2048]{0,1:T(8,128)}, u32[]{:S(2)}, u32[]{:S(2)}) collective-permute-start(f32[128,2048]{0,1:T(8,128)} %bitcast.8), channel_id=1, source_target_pairs={{0,16},{16,0},{32,48},{48,32},{64,80},{80,64},{96,112},{112,96},{1... | collective-permute-start | bytes 3145736 | tf_op jit(solution)/shard_map/ppermute | solution.py:21
  42.7 177.7 %copy-start.89 = (s32[24]{0:T(128)}, s32[24]{0:T(128)S(1)}, u32[]{:S(2)}) copy-start(s32[24]{0:T(128)S(1)} %get-tuple-element.186) | copy-start | bytes 292
  57.3 53.5 %all-to-all-start = ((f32[2,128,16,192]{1,3,0,2:T(8,128)}), f32[2,128,16,192]{1,3,0,2:T(8,128)S(1)}, u32[]{:S(2)}, u32[]{:S(2)}) async-start(f32[2,128,16,192]{1,3,0,2:T(8,128)} %pad_maximum_fusion), calls=%async_computation | async-start | bytes 6291456 | tf_op jit(solution)/shard_map/all_to_all | solution.py:188
  64.2 152.3 %all-reduce.30.cloned.1.call-start = ((), (), s32[]{:S(2)}) async-start(), calls=%async_computation.4 | async-start | bytes 524288 | tf_op jit(solution)/shard_map/psum | solution.py:168
  154.8 116.6 %all-gather.5.cloned.1.call-start = ((), (), s32[]{:S(2)}) async-start(), calls=%async_computation.5 | async-start | bytes 4456448 | tf_op jit(solution)/shard_map/all_gather | solution.py:198
  218.9 327.8 %all-gather.7.cloned.1.call-start = ((), (), s32[]{:S(2)}) async-start(), calls=%async_computation.6 | async-start | bytes 8912896 | tf_op jit(solution)/shard_map/all_gather | solution.py:200
  219.8 506.3 %all-gather.9.cloned.1.call-start = ((), (), s32[]{:S(2)}) async-start(), calls=%async_computation.7 | async-start | bytes 4456448 | tf_op jit(solution)/shard_map/all_gather | solution.py:198
  322.6 52.3 %copy-start.51 = (f32[128,128]{1,0:T(8,128)}, f32[128,128]{1,0:T(8,128)S(1)}, u32[]{:S(2)}) copy-start(f32[128,128]{1,0:T(8,128)S(1)} %copy.426) | copy-start | bytes 196612
  324.4 25.6 %copy-start.44 = (f32[128,128]{1,0:T(8,128)}, f32[128,128]{1,0:T(8,128)S(1)}, u32[]{:S(2)}) copy-start(f32[128,128]{1,0:T(8,128)S(1)} %convolution_negate_fusion.13) | copy-start | bytes 196612
  325.8 54.7 %copy-start.3 = (f32[256,256]{0,1:T(8,128)}, f32[256,256]{0,1:T(8,128)S(1)}, u32[]{:S(2)}) copy-start(f32[256,256]{0,1:T(8,128)S(1)} %fusion.133) | copy-start | bytes 786436
  350.3 29.6 %copy-start.45 = (f32[128,128]{1,0:T(8,128)S(1)}, f32[128,128]{1,0:T(8,128)}, u32[]{:S(2)}) copy-start(f32[128,128]{1,0:T(8,128)} %copy-done.44) | copy-start | bytes 196612
  350.5 30.0 %copy-start.16 = (f32[128,128]{0,1:T(8,128)}, f32[128,128]{0,1:T(8,128)S(1)}, u32[]{:S(2)}) copy-start(f32[128,128]{0,1:T(8,128)S(1)} %fusion.170) | copy-start | bytes 196612
  375.0 6.2 copy-start.60
  375.0 4.9 copy-start.52
  375.0 6.1 copy-start.22
  379.9 5.5 copy-start.12
  385.4 156.4 %copy-start.1 = (f32[512,512]{0,1:T(8,128)}, f32[512,512]{0,1:T(8,128)S(1)}, u32[]{:S(2)}) copy-start(f32[512,512]{0,1:T(8,128)S(1)} %fusion.51) | copy-start | bytes 3145732
  535.5 5.0 copy-start.63
  535.5 5.3 copy-start.5
  535.5 5.3 copy-start.47
  535.5 5.3 copy-start.53
  535.5 5.9 copy-start.68
  535.5 5.9 copy-start.84
  535.5 6.3 copy-start.23
  535.5 6.3 copy-start.27
  535.5 6.3 copy-start.32
  535.5 6.3 copy-start.57
  535.6 6.3 copy-start.61
  536.8 6.9 copy-start.65
  541.9 4.8 copy-start.85
  582.9 9.7 copy-start
  582.9 11.0 %copy-start.88 = (s32[24]{0:T(128)S(1)}, s32[24]{0:T(128)}, u32[]{:S(2)}) copy-start(s32[24]{0:T(128)} %compare_select_fusion.1) | copy-start | bytes 292
  582.9 11.0 %copy-start.90 = (s32[24]{0:T(128)S(1)}, s32[24]{0:T(128)}, u32[]{:S(2)}) copy-start(s32[24]{0:T(128)} %copy-done.89) | copy-start | bytes 292
  592.6 24.2 %collective-permute-start.1 = (f32[128,2048]{1,0:T(8,128)}, f32[128,2048]{1,0:T(8,128)}, u32[]{:S(2)}, u32[]{:S(2)}) collective-permute-start(f32[128,2048]{1,0:T(8,128)} %convolution_subtract_fusion.1), channel_id=1, source_target_pairs={{0,32},{32,0},{16,48},{48,16},{64,96},{96,64},{80,112},{112,80},{1... | collective-permute-start | bytes 3145736 | tf_op jit(solution)/shard_map/ppermute | solution.py:21
  673.7 6.8 copy-start.17
  673.7 12.4 %copy-start.2 = (f32[512,512]{0,1:T(8,128)S(1)}, f32[512,512]{0,1:T(8,128)}, u32[]{:S(2)}) copy-start(f32[512,512]{0,1:T(8,128)} %copy-done.1) | copy-start | bytes 3145732
  674.5 329.2 %all-gather.11.cloned.1.call-start = ((), (), s32[]{:S(2)}) async-start(), calls=%async_computation.8 | async-start | bytes 8912896 | tf_op jit(solution)/shard_map/all_gather | solution.py:200
  678.7 9.7 copy-start.75
  686.1 6.0 copy-start.70
  687.5 4.0 copy-start.78
  687.5 4.0 copy-start.79
  687.5 4.0 copy-start.83
  783.0 54.4 %copy-start.50 = (f32[128,128]{1,0:T(8,128)S(1)}, f32[128,128]{1,0:T(8,128)}, u32[]{:S(2)}) copy-start(f32[128,128]{1,0:T(8,128)} %copy-done.49) | copy-start | bytes 196612
  806.8 32.2 %copy-start.20 = (f32[128,256]{1,0:T(8,128)}, f32[128,256]{1,0:T(8,128)S(1)}, u32[]{:S(2)}) copy-start(f32[128,256]{1,0:T(8,128)S(1)} %concatenate.333) | copy-start | bytes 393220
  832.4 6.1 copy-start.58
  988.6 4.6 copy-start.71
  989.6 11.3 %copy-start.64 = (f32[256,512]{1,0:T(8,128)}, f32[256,512]{1,0:T(8,128)S(1)}, u32[]{:S(2)}) copy-start(f32[256,512]{1,0:T(8,128)S(1)} %concatenate.353) | copy-start | bytes 1572868
  990.8 3.0 copy-start.9
  990.8 3.0 copy-start.10
  990.8 3.0 copy-start.11
  990.8 3.0 copy-start.28
  990.8 3.0 copy-start.38
  990.8 3.0 copy-start.39
  990.8 3.0 copy-start.69
  990.8 3.0 copy-start.72
  990.8 3.0 copy-start.73
  990.9 3.0 copy-start.74
  993.9 3.4 copy-start.34
  994.0 3.7 copy-start.62
  995.4 3.2 copy-start.66
  995.4 3.2 copy-start.82
  999.0 4.8 copy-start.67
  1034.4 9.7 copy-start.15
  (36 other events, 59.1 us)
Sparse Core Ops, SparseCore 0:
  41.0 113.6 reduce-scatter.1
  157.1 59.3 all-reduce.29
  219.2 52.1 all-gather.4
  274.0 70.5 all-gather.6
  674.7 51.4 all-gather.8
  728.2 70.6 all-gather.10
where the time goes:
time: 1060 us; the launch traced here: 1050 us
  other arithmetic  460 us (43%)
  waiting for transfers between devices  241 us (23%)
  matrix products  169 us (16%)
  local copies, waits for them, and re-layouts  113 us (11%)
  blocking collectives  42.2 us (4%)
  between operations  16.8 us (2%)
    another operation x48, other arithmetic, cholesky_inverse(): lower = jnp.linalg.cholesky(matrix)  214 us
    another operation x32, other arithmetic, cholesky_inverse(): jax.scipy.linalg.solve_triangular(lower, identity, lower=True)  192 us
    all_gather x2, waiting for transfers between devices, shards(): pivot_all = lax.all_gather(sep_front[:, :S], 'inner', axis=0, tiled=True)  79.9 us
    dot_general x2, matrix products, shards(): jnp.dot(coupling_all, pivot_inverse.T, precision=HIGHEST, preferred_eleme...  66.8 us
    psum x1, waiting for transfers between devices, shards(): lax.psum(lax.psum_scatter(per_front, 'inner', scatter_dimension=1, tiled=...  58.7 us
    all_to_all x1, waiting for transfers between devices, shards(): lax.all_to_all(outgoing, 'inner', split_axis=2, concat_axis=1, tiled=True)  46.5 us
    all_to_all x1, blocking collectives, shards(): lax.all_to_all(outgoing, 'inner', split_axis=2, concat_axis=1, tiled=True)  42.2 us
    reduce_scatter x1, waiting for transfers between devices, shards(): lax.psum_scatter(per_front, 'inner', scatter_dimension=1, tiled=True)  39.2 us
  transfers between devices with their start and end apart: 9, of which 6 were waited for; matrix products, arithmetic and copies ran while one was open for 59% of the time, Pallas kernels for 0%

commit v1 on v0

--- a/solution.py
+++ b/solution.py
@@ -195,7 +195,10 @@
         block_now = lax.dynamic_slice_in_dim(sep_front, block_start, BLK, 1)
         sep_front = lax.dynamic_update_slice_in_dim(sep_front, block_now + obs_rows, block_start, 1)
         front_offset = front_offset + (group_count >> level_index + 1)
-        pivot_all = lax.all_gather(sep_front[:, :S], "inner", axis=0, tiled=True)
+        pivot_all = jnp.concatenate(
+            lax.all_to_all(jnp.stack([sep_front[:, :S]] * lax.axis_size("inner")), "inner", 0, 0),
+            axis=0,
+        )
         border_front = front_rows[sep_rows:]
         coupling_all = lax.all_gather(border_front[:, :S], "inner", axis=0, tiled=True)
         pivot_lower, pivot_inverse = cholesky_inverse(pivot_all, BLK)

time: 1060 us -> 1110 us (1.047)
  the two profiles are of different devices: /device:TPU:1 before, /device:TPU:96 now
where the time goes in v1:
time: 1110 us; the launch traced here: 1100 us
  other arithmetic  464 us (42%)
  waiting for transfers between devices  305 us (27%)
  matrix products  169 us (15%)
  local copies, waits for them, and re-layouts  113 us (10%)
  starting transfers between devices  31.2 us (3%)
  between operations  16.7 us (2%)
    another operation x48, other arithmetic, cholesky_inverse(): lower = jnp.linalg.cholesky(matrix)  214 us
    another operation x32, other arithmetic, cholesky_inverse(): jax.scipy.linalg.solve_triangular(lower, identity, lower=True)  192 us
    all_to_all x2, waiting for transfers between devices, shards(): lax.all_to_all(jnp.stack([sep_front[:, :S]] * lax.axis_size('inner')), 'i...  107 us
    all_to_all x2, waiting for transfers between devices, shards(): lax.all_to_all(outgoing, 'inner', split_axis=2, concat_axis=1, tiled=True)  92.9 us
    dot_general x2, matrix products, shards(): jnp.dot(coupling_all, pivot_inverse.T, precision=HIGHEST, preferred_eleme...  66.8 us
    psum x1, waiting for transfers between devices, shards(): lax.psum(lax.psum_scatter(per_front, 'inner', scatter_dimension=1, tiled=...  56.7 us
    reduce_scatter x1, waiting for transfers between devices, shards(): lax.psum_scatter(per_front, 'inner', scatter_dimension=1, tiled=True)  29.8 us
  transfers between devices with their start and end apart: 10, of which 7 were waited for; matrix products, arithmetic and copies ran while one was open for 57% of the time, Pallas kernels for 0%

profile of v1, /device:TPU:96, one launch (start us, length us, event | category | flops | bytes accessed | tf_op | source)
XLA Modules:
  0.0 1097.9 jit_solution(14751144831044171565)
XLA Ops:
  7.2 2.5 copy.328
  9.7 25.9 %while.14 = (s32[]{:T(128)}, f32[48,128,128]{2,1,0:T(8,128)S(1)}, s32[2048]{0:T(1024)}, bf16[2048,128]{1,0:T(8,128)(2,1)}, s32[]{:T(128)}, /*index=5*/s32[]{:T(128)}, s32[]{:T(128)}, s32[]{:T(128)}) while((s32[]{:T(128)}, f32[48,128,128]{2,1,0:T(8,128)S(1)}, s32[2048]{0:T(1024)}, bf16[2048,128]{1,0:T(8,128)(2,1)}, s32[]{:T(128)}, ...), condition=%wide.region_5.8_spmd.clone, body=%wide.region_4.7_spmd.clone.sunk | while | flops 405823488 | bytes 6737053 | solution.py:164
  53.6 7.1 all-to-all-start
  60.7 53.7 %all-to-all-done = f32[2,128,16,192]{1,3,0,2:T(8,128)S(1)} async-done(((f32[2,128,16,192]{1,3,0,2:T(8,128)}), f32[2,128,16,192]{1,3,0,2:T(8,128)S(1)}, u32[]{:S(2)}, u32[]{:S(2)}) %all-to-all-start) | async-done | bytes 3145760 | tf_op jit(solution)/shard_map/all_to_all | solution.py:188
  119.1 29.8 %reduce-scatter.2.cloned.1.call-done = f32[6,64,128]{2,1,0:T(8,128)} async-done(((f32[6,1024,128]{2,1,0:T(8,128)}), f32[6,64,128]{2,1,0:T(8,128)}) %reduce-scatter.2.cloned.1.call-update) | async-done | bytes 196624 | tf_op jit(solution)/shard_map/reduce_scatter | solution.py:169
  148.9 2.8 bitcast_bitcast_fusion.1
  151.8 56.7 %all-reduce.30.cloned.1.call-done = f32[6,64,128]{2,1,0:T(8,128)} async-done(((f32[6,64,128]{2,1,0:T(8,128)}), f32[6,64,128]{2,1,0:T(8,128)}) %all-reduce.30.cloned.1.call-update) | async-done | bytes 196624 | tf_op jit(solution)/shard_map/psum | solution.py:168
  209.3 2.5 stack.31
  211.8 6.9 all-to-all-start.1
  220.5 71.9 %all-to-all-done.1 = f32[16,64,1024]{2,1,0:T(8,128)} async-done(((f32[16,64,1024]{2,1,0:T(8,128)}), f32[16,64,1024]{2,1,0:T(8,128)}, u32[]{:S(2)}, u32[]{:S(2)}) %all-to-all-start.1) | async-done | bytes 4194336 | tf_op jit(solution)/shard_map/all_to_all | solution.py:199
  294.2 2.3 slice.307
  297.6 11.7 %cholesky.254 = f32[128,128]{1,0:T(8,128)S(1)} custom-call(f32[128,128]{1,0:T(8,128)S(1)} %get-tuple-element.162), custom_call_target="Cholesky" | custom-call | tf_op jit(solution)/shard_map/jit(cholesky)/cholesky | solution.py:93
  311.3 9.8 custom-call.21
  322.9 11.7 %cholesky.265 = f32[128,128]{1,0:T(8,128)S(1)} custom-call(f32[128,128]{1,0:T(8,128)S(1)} %fusion.203), custom_call_target="Cholesky" | custom-call | tf_op jit(solution)/shard_map/jit(cholesky)/cholesky | solution.py:93
  336.6 10.0 custom-call.22
  349.8 11.7 %cholesky.276 = f32[128,128]{1,0:T(8,128)S(1)} custom-call(f32[128,128]{1,0:T(8,128)S(1)} %fusion.201), custom_call_target="Cholesky" | custom-call | tf_op jit(solution)/shard_map/jit(cholesky)/cholesky | solution.py:93
  363.5 9.8 custom-call.23
  374.2 12.1 %cholesky.287 = f32[128,128]{1,0:T(8,128)S(1)} custom-call(f32[128,128]{1,0:T(8,128)S(1)} %fusion.199), custom_call_target="Cholesky" | custom-call | tf_op jit(solution)/shard_map/jit(cholesky)/cholesky | solution.py:93
  388.3 9.8 custom-call.24
  398.5 2.6 copy.447
  404.4 3.1 fusion.51
  413.5 12.7 %cholesky.298 = f32[128,128]{1,0:T(8,128)S(1)} custom-call(f32[128,128]{1,0:T(8,128)} %fusion.197), custom_call_target="Cholesky" | custom-call | tf_op jit(solution)/shard_map/jit(cholesky)/cholesky | solution.py:93
  428.1 11.3 %custom-call.25 = f32[1,128,128]{1,2,0:T(8,128)} custom-call(f32[1,128,128]{2,1,0:T(8,128)} %get-tuple-element.149), custom_call_target="InvertDiagBlocksLowerTriangular" | custom-call | tf_op jit(solution)/shard_map/jit(_solve_triangular)/triangular_solve | solution.py:95
  447.1 13.2 %cholesky.309 = f32[128,128]{1,0:T(8,128)} custom-call(f32[128,128]{1,0:T(8,128)} %fusion.195), custom_call_target="Cholesky" | custom-call | tf_op jit(solution)/shard_map/jit(cholesky)/cholesky | solution.py:93
  463.9 11.3 %custom-call.26 = f32[1,128,128]{1,2,0:T(8,128)} custom-call(f32[1,128,128]{2,1,0:T(8,128)} %get-tuple-element.147), custom_call_target="InvertDiagBlocksLowerTriangular" | custom-call | tf_op jit(solution)/shard_map/jit(_solve_triangular)/triangular_solve | solution.py:95
  489.3 13.6 %cholesky.320 = f32[128,128]{1,0:T(8,128)} custom-call(f32[128,128]{1,0:T(8,128)} %fusion.193), custom_call_target="Cholesky" | custom-call | tf_op jit(solution)/shard_map/jit(cholesky)/cholesky | solution.py:93
  506.5 11.3 %custom-call.27 = f32[1,128,128]{1,2,0:T(8,128)} custom-call(f32[1,128,128]{2,1,0:T(8,128)} %get-tuple-element.145), custom_call_target="InvertDiagBlocksLowerTriangular" | custom-call | tf_op jit(solution)/shard_map/jit(_solve_triangular)/triangular_solve | solution.py:95
  526.1 13.2 %cholesky.331 = f32[128,128]{1,0:T(8,128)} custom-call(f32[128,128]{1,0:T(8,128)} %fusion.191), custom_call_target="Cholesky" | custom-call | tf_op jit(solution)/shard_map/jit(cholesky)/cholesky | solution.py:93
  542.9 11.3 %custom-call.28 = f32[1,128,128]{1,2,0:T(8,128)} custom-call(f32[1,128,128]{2,1,0:T(8,128)} %get-tuple-element.143), custom_call_target="InvertDiagBlocksLowerTriangular" | custom-call | tf_op jit(solution)/shard_map/jit(_solve_triangular)/triangular_solve | solution.py:95
  558.7 2.4 select_maximum_fusion.6
  565.7 2.9 convolution_negate_fusion.1
  568.6 36.2 %fusion.12 = f32[2048,1024]{1,0:T(8,128)S(1)} fusion(f32[2048,1024]{1,0:T(8,128)} %all-gather.3.cloned.1.call-done, f32[512,512]{1,0:T(8,128)S(1)} %copy-done.38, f32[128,128]{1,0:T(8,128)S(1)} %copy-done.86, f32[128,128]{1,0:T(8,128)} %copy-done.82, f32[128,256]{1,0:T(8,128)} %concatenate.310, f32[256,256]{1,0:T(8,128)} %copy-done.78, ...), kind=kOutput, calls=%fused_computation.29 | convolution fusion | flops 25778192384 | bytes 19922944 | tf_op jit(solution)/shard_map/dot_general | solution.py:205
  604.8 9.7 convolution_subtract_fusion.1
  621.3 18.3 %collective-permute-done.1 = f32[128,2048]{1,0:T(8,128)} collective-permute-done((f32[128,2048]{1,0:T(8,128)}, f32[128,2048]{1,0:T(8,128)}, u32[]{:S(2)}, u32[]{:S(2)}) %collective-permute-start.1) | collective-permute-done | bytes 1048608 | tf_op jit(solution)/shard_map/ppermute | solution.py:21
  648.1 11.0 all-to-all-start.2
  659.0 39.2 %all-to-all-done.2 = f32[2,128,16,192]{1,3,0,2:T(8,128)S(1)} async-done(((f32[2,128,16,192]{1,3,0,2:T(8,128)}), f32[2,128,16,192]{1,3,0,2:T(8,128)S(1)}, u32[]{:S(2)}, u32[]{:S(2)}) %all-to-all-start.2) | async-done | bytes 3145760 | tf_op jit(solution)/shard_map/all_to_all | solution.py:188
  702.9 2.8 bitcast_bitcast_fusion
  706.6 2.5 stack.36
  709.1 5.8 all-to-all-start.3
  732.6 2.5 pad_select_fusion.1
  737.0 34.9 %all-to-all-done.3 = f32[16,64,1024]{2,1,0:T(8,128)} async-done(((f32[16,64,1024]{2,1,0:T(8,128)}), f32[16,64,1024]{2,1,0:T(8,128)}, u32[]{:S(2)}, u32[]{:S(2)}) %all-to-all-start.3) | async-done | bytes 4194336 | tf_op jit(solution)/shard_map/all_to_all | solution.py:199
  773.7 2.4 slice.335
  777.1 11.7 %cholesky.342 = f32[128,128]{1,0:T(8,128)S(1)} custom-call(f32[128,128]{1,0:T(8,128)S(1)} %get-tuple-element.160), custom_call_target="Cholesky" | custom-call | tf_op jit(solution)/shard_map/jit(cholesky)/cholesky | solution.py:93
  790.8 9.8 custom-call.29
  803.2 11.9 %cholesky.353 = f32[128,128]{1,0:T(8,128)S(1)} custom-call(f32[128,128]{1,0:T(8,128)S(1)} %fusion.187), custom_call_target="Cholesky" | custom-call | tf_op jit(solution)/shard_map/jit(cholesky)/cholesky | solution.py:93
  817.1 9.8 custom-call.30
  831.0 11.7 %cholesky.364 = f32[128,128]{1,0:T(8,128)S(1)} custom-call(f32[128,128]{1,0:T(8,128)S(1)} %fusion.185), custom_call_target="Cholesky" | custom-call | tf_op jit(solution)/shard_map/jit(cholesky)/cholesky | solution.py:93
  844.5 9.8 custom-call.31
  856.0 12.1 %cholesky.375 = f32[128,128]{1,0:T(8,128)S(1)} custom-call(f32[128,128]{1,0:T(8,128)S(1)} %fusion.183), custom_call_target="Cholesky" | custom-call | tf_op jit(solution)/shard_map/jit(cholesky)/cholesky | solution.py:93
  870.1 9.8 custom-call.32
  880.3 2.6 copy.451
  885.2 3.1 fusion.47
  889.7 3.1 convolution_subtract_fusion.2
  894.7 11.9 %cholesky.386 = f32[128,128]{1,0:T(8,128)S(1)} custom-call(f32[128,128]{1,0:T(8,128)S(1)} %fusion.181), custom_call_target="Cholesky" | custom-call | tf_op jit(solution)/shard_map/jit(cholesky)/cholesky | solution.py:93
  908.5 10.4 custom-call.33
  926.7 13.2 %cholesky.397 = f32[128,128]{1,0:T(8,128)} custom-call(f32[128,128]{1,0:T(8,128)} %fusion.179), custom_call_target="Cholesky" | custom-call | tf_op jit(solution)/shard_map/jit(cholesky)/cholesky | solution.py:93
  943.6 11.3 %custom-call.34 = f32[1,128,128]{1,2,0:T(8,128)} custom-call(f32[1,128,128]{2,1,0:T(8,128)} %get-tuple-element.131), custom_call_target="InvertDiagBlocksLowerTriangular" | custom-call | tf_op jit(solution)/shard_map/jit(_solve_triangular)/triangular_solve | solution.py:95
  969.8 12.5 %cholesky.408 = f32[128,128]{1,0:T(8,128)S(1)} custom-call(f32[128,128]{1,0:T(8,128)} %fusion.177), custom_call_target="Cholesky" | custom-call | tf_op jit(solution)/shard_map/jit(cholesky)/cholesky | solution.py:93
  984.4 10.6 custom-call.35
  1002.6 13.2 %cholesky.419 = f32[128,128]{1,0:T(8,128)} custom-call(f32[128,128]{1,0:T(8,128)} %fusion.175), custom_call_target="Cholesky" | custom-call | tf_op jit(solution)/shard_map/jit(cholesky)/cholesky | solution.py:93
  1020.0 11.3 %custom-call.36 = f32[1,128,128]{1,2,0:T(8,128)} custom-call(f32[1,128,128]{2,1,0:T(8,128)} %get-tuple-element.127), custom_call_target="InvertDiagBlocksLowerTriangular" | custom-call | tf_op jit(solution)/shard_map/jit(_solve_triangular)/triangular_solve | solution.py:95
  1046.9 2.8 convolution_negate_fusion
  1049.7 30.6 %fusion.10 = f32[2048,1024]{1,0:T(8,128)S(1)} fusion(f32[2048,1024]{1,0:T(8,128)} %all-gather.5.cloned.1.call-done, f32[512,512]{1,0:T(8,128)S(1)} %copy-done.37, f32[128,128]{1,0:T(8,128)} %copy.413, f32[128,128]{1,0:T(8,128)} %copy-done.81, f32[128,256]{1,0:T(8,128)S(1)} %copy-done.68, f32[256,256]{1,0:T(8,128)} %copy-done.77, f32[256,512]{1,0:T(8,128)} %copy-done.65, ...), kind=kOutput, calls=%fused_computation.23 | convolution fusion | flops 25778192384 | bytes 19922944 | tf_op jit(solution)/shard_map/dot_general | solution.py:205
  1080.4 9.7 fusion.38
  (510 shorter events, 251.3 us)
Async XLA Ops:
  7.2 141.7 %reduce-scatter.2.cloned.1.call-start = ((), (), s32[]{:S(2)}) async-start(), calls=%async_computation.5 | async-start | bytes 3342336 | tf_op jit(solution)/shard_map/reduce_scatter | solution.py:169
  9.7 34.9 %collective-permute-start = (f32[128,2048]{0,1:T(8,128)}, f32[128,2048]{0,1:T(8,128)}, u32[]{:S(2)}, u32[]{:S(2)}) collective-permute-start(f32[128,2048]{0,1:T(8,128)} %bitcast.8), channel_id=1, source_target_pairs={{0,16},{16,0},{32,48},{48,32},{64,80},{80,64},{96,112},{112,96},{1... | collective-permute-start | bytes 3145736 | tf_op jit(solution)/shard_map/ppermute | solution.py:21
  35.7 3.3 copy-start.87
  39.1 180.7 %copy-start.89 = (s32[24]{0:T(128)}, s32[24]{0:T(128)S(1)}, u32[]{:S(2)}) copy-start(s32[24]{0:T(128)S(1)} %get-tuple-element.175) | copy-start | bytes 292
  53.6 60.9 %all-to-all-start = ((f32[2,128,16,192]{1,3,0,2:T(8,128)}), f32[2,128,16,192]{1,3,0,2:T(8,128)S(1)}, u32[]{:S(2)}, u32[]{:S(2)}) async-start(f32[2,128,16,192]{1,3,0,2:T(8,128)} %pad_maximum_fusion), calls=%async_computation | async-start | bytes 6291456 | tf_op jit(solution)/shard_map/all_to_all | solution.py:188
  60.6 147.9 %all-reduce.30.cloned.1.call-start = ((), (), s32[]{:S(2)}) async-start(), calls=%async_computation.6 | async-start | bytes 393216 | tf_op jit(solution)/shard_map/psum | solution.py:168
  211.8 80.6 %all-to-all-start.1 = ((f32[16,64,1024]{2,1,0:T(8,128)}), f32[16,64,1024]{2,1,0:T(8,128)}, u32[]{:S(2)}, u32[]{:S(2)}) async-start(f32[16,64,1024]{2,1,0:T(8,128)} %stack.31), calls=%async_computation.2 | async-start | bytes 8388608 | tf_op jit(solution)/shard_map/all_to_all | solution.py:199
  218.7 349.9 %all-gather.3.cloned.1.call-start = ((), (), s32[]{:S(2)}) async-start(), calls=%async_computation.7 | async-start | bytes 8912896 | tf_op jit(solution)/shard_map/all_gather | solution.py:203
  346.9 51.4 %copy-start.52 = (f32[128,128]{1,0:T(8,128)}, f32[128,128]{1,0:T(8,128)S(1)}, u32[]{:S(2)}) copy-start(f32[128,128]{1,0:T(8,128)S(1)} %copy.343) | copy-start | bytes 196612
  347.7 25.6 %copy-start.47 = (f32[128,128]{1,0:T(8,128)}, f32[128,128]{1,0:T(8,128)S(1)}, u32[]{:S(2)}) copy-start(f32[128,128]{1,0:T(8,128)S(1)} %convolution_negate_fusion.13) | copy-start | bytes 196612
  349.1 53.6 %copy-start.4 = (f32[256,256]{0,1:T(8,128)}, f32[256,256]{0,1:T(8,128)S(1)}, u32[]{:S(2)}) copy-start(f32[256,256]{0,1:T(8,128)S(1)} %fusion.133) | copy-start | bytes 786436
  373.6 27.5 %copy-start.48 = (f32[128,128]{1,0:T(8,128)S(1)}, f32[128,128]{1,0:T(8,128)}, u32[]{:S(2)}) copy-start(f32[128,128]{1,0:T(8,128)} %copy-done.47) | copy-start | bytes 196612
  373.8 33.7 %copy-start.17 = (f32[128,128]{0,1:T(8,128)}, f32[128,128]{0,1:T(8,128)S(1)}, u32[]{:S(2)}) copy-start(f32[128,128]{0,1:T(8,128)S(1)} %fusion.170) | copy-start | bytes 196612
  398.5 4.8 copy-start.61
  398.5 4.2 copy-start.53
  398.5 4.8 copy-start.23
  401.1 6.4 copy-start.13
  407.6 156.1 %copy-start.2 = (f32[512,512]{0,1:T(8,128)}, f32[512,512]{0,1:T(8,128)S(1)}, u32[]{:S(2)}) copy-start(f32[512,512]{0,1:T(8,128)S(1)} %fusion.51) | copy-start | bytes 3145732
  557.4 4.9 copy-start.64
  557.4 5.2 copy-start.6
  557.4 5.2 copy-start.46
  557.4 5.2 copy-start.54
  557.4 5.8 copy-start.69
  557.4 5.8 copy-start.85
  557.6 6.0 copy-start.24
  557.6 6.0 copy-start.28
  557.7 6.0 copy-start.33
  557.7 6.0 copy-start.58
  557.7 6.0 copy-start.62
  558.7 6.9 copy-start.66
  563.7 4.9 copy-start.86
  604.8 9.7 copy-start.1
  604.8 9.7 copy-start.88
  604.8 9.7 copy-start.90
  614.5 25.1 %collective-permute-start.1 = (f32[128,2048]{1,0:T(8,128)}, f32[128,2048]{1,0:T(8,128)}, u32[]{:S(2)}, u32[]{:S(2)}) collective-permute-start(f32[128,2048]{1,0:T(8,128)} %convolution_subtract_fusion.1), channel_id=1, source_target_pairs={{0,32},{32,0},{16,48},{48,16},{64,96},{96,64},{80,112},{112,80},{1... | collective-permute-start | bytes 3145736 | tf_op jit(solution)/shard_map/ppermute | solution.py:21
  648.1 50.1 %all-to-all-start.2 = ((f32[2,128,16,192]{1,3,0,2:T(8,128)}), f32[2,128,16,192]{1,3,0,2:T(8,128)S(1)}, u32[]{:S(2)}, u32[]{:S(2)}) async-start(f32[2,128,16,192]{1,3,0,2:T(8,128)} %pad_maximum_fusion.1), calls=%async_computation.3 | async-start | bytes 6291456 | tf_op jit(solution)/shard_map/all_to_all | solution.py:188
  709.1 62.7 %all-to-all-start.3 = ((f32[16,64,1024]{2,1,0:T(8,128)}), f32[16,64,1024]{2,1,0:T(8,128)}, u32[]{:S(2)}, u32[]{:S(2)}) async-start(f32[16,64,1024]{2,1,0:T(8,128)} %stack.36), calls=%async_computation.4 | async-start | bytes 8388608 | tf_op jit(solution)/shard_map/all_to_all | solution.py:199
  714.9 5.9 copy-start.18
  715.0 11.6 %copy-start.3 = (f32[512,512]{0,1:T(8,128)S(1)}, f32[512,512]{0,1:T(8,128)}, u32[]{:S(2)}) copy-start(f32[512,512]{0,1:T(8,128)} %copy-done.2) | copy-start | bytes 3145732
  715.0 334.7 %all-gather.5.cloned.1.call-start = ((), (), s32[]{:S(2)}) async-start(), calls=%async_computation.8 | async-start | bytes 8912896 | tf_op jit(solution)/shard_map/all_gather | solution.py:203
  719.1 9.8 copy-start.76
  726.5 6.0 copy-start.71
  727.9 4.0 copy-start.79
  727.9 4.0 copy-start.80
  727.9 4.0 copy-start.84
  830.8 52.0 %copy-start.51 = (f32[128,128]{1,0:T(8,128)S(1)}, f32[128,128]{1,0:T(8,128)}, u32[]{:S(2)}) copy-start(f32[128,128]{1,0:T(8,128)} %copy-done.50) | copy-start | bytes 196612
  854.6 33.7 %copy-start.21 = (f32[128,256]{1,0:T(8,128)}, f32[128,256]{1,0:T(8,128)S(1)}, u32[]{:S(2)}) copy-start(f32[128,256]{1,0:T(8,128)S(1)} %concatenate.333) | copy-start | bytes 393220
  880.2 3.8 copy-start.59
  1034.6 4.6 copy-start.72
  1035.6 11.3 %copy-start.65 = (f32[256,512]{1,0:T(8,128)}, f32[256,512]{1,0:T(8,128)S(1)}, u32[]{:S(2)}) copy-start(f32[256,512]{1,0:T(8,128)S(1)} %concatenate.353) | copy-start | bytes 1572868
  1036.7 3.0 copy-start.10
  1036.7 3.0 copy-start.11
  1036.7 3.0 copy-start.12
  1036.7 3.0 copy-start.29
  1036.7 3.0 copy-start.39
  1036.7 3.0 copy-start.40
  1036.7 3.0 copy-start.70
  1036.8 3.0 copy-start.73
  1039.9 3.4 copy-start.35
  1039.9 3.7 copy-start.63
  1041.3 3.2 copy-start.67
  1041.3 3.2 copy-start.83
  1044.9 4.8 copy-start.68
  1080.4 9.8 copy-start.16
  (37 other events, 63.1 us)
Sparse Core Ops, SparseCore 0:
  37.5 111.3 reduce-scatter.1
  151.2 57.3 all-reduce.29
  222.2 107.4 all-gather.2
  732.0 89.3 all-gather.4
